TPU v7x, 128 devices: a whole 4x4x4 slice. The times are simulated.
128 devices in a mesh: tok: 16 (over y, z), own: 8 (over x, core).
Axes of the slice: x: 4, y: 4, z: 4, core: 2. Of those that a mesh axis runs over, the one named last changes fastest.
Arguments:
- tokens: bfloat16 [16384, 1152], P(('tok', 'own')), may hold values from -6 to 6
- norm_gain: bfloat16 [1152], replicated, may hold values from 0.099609375 to 1.8984375
- w_query: bfloat16 [1152, 1152], replicated, as said below
- w_key: bfloat16 [1152, 384], replicated, as said below
- w_value: bfloat16 [1152, 384], replicated, may hold values from -0.1875 to 0.1875
- w_output: bfloat16 [1152, 1152], replicated, may hold values from -0.1875 to 0.1875
- qkv_in: bfloat16 [64, 48, 1152], P('own', None, 'tok'), may hold values from -0.1875 to 0.1875
- q_out: bfloat16 [64, 16, 1152], P('own', None, 'tok'), may hold values from -1.5 to 1.5
- kv_out: bfloat16 [64, 32, 384], P('own', None, 'tok'), may hold values from -1.5 to 1.5
- o_in: bfloat16 [64, 16, 1152], P('own', None, 'tok'), may hold values from -0.1875 to 0.1875
- o_out: bfloat16 [64, 16, 1152], P('own', None, 'tok'), may hold values from -1.5 to 1.5
- lengths: int32 [64], replicated, may hold values from 32 to 1536, as said below
- prompt_adapter: int32 [64], replicated, may hold values from 0 to 63
- adapter_slot: int32 [64], replicated, may hold values from 0 to 63, each once
Outputs:
- mixed: bfloat16 [16384, 1152], P(('tok', 'own'))
- kv_cache: bfloat16 [16384, 768], P(('tok', 'own'))
Inputs may be any that keep to these rules, and one draw needn't show every extreme that they name: `w_query`: entries lie within 6 / sqrt(1152) of zero. `w_key`: entries lie within 6 / sqrt(1152) of zero. `lengths`: lengths sum to 16384; exactly 8 prompts are 1536 long; the others hold 32 to 128 tokens, and one of them exactly 32. `adapter_slot`: each slot appears once; slot s is row s of the adapter tables, held by own index s // 8.
All inputs are finite; a program needn't handle non-finite values.
Results may differ from a plain program's by a relative error of at most 0.02.
Values may be sent and summed in bfloat16 or wider, within the bound.
No kernel may reach another device: no remote copies, remote signals or barrier semaphores. Data moves between devices by JAX's collectives and lax.ppermute only.
A program may use at most 128 MiB of HBM per device.

v0:
```python
import math
import jax
import jax.numpy as jnp
from jax import lax
from jax.sharding import PartitionSpec as P

D = 1152
HEADS = 18
KV_HEADS = 6
HEAD_WIDTH = 64
RANK = 16
REACH = 12
KVW = 384
SEG_DEV = 5
EPS = 1e-05
THETA = 10000.0


def from_behind(block, axis, distance):
    devices = range(lax.axis_size(axis))
    route = [(i - distance, i) for i in devices if i - distance in devices]
    return lax.ppermute(block, axis, route)


def rms_norm(row_block, gain_vec):
    widened = row_block.astype(jnp.float32)
    inverse_rms = lax.rsqrt(jnp.mean(widened * widened, axis=-1, keepdims=True) + EPS)
    return (widened * inverse_rms * gain_vec.astype(jnp.float32)).astype(jnp.bfloat16)


def prompt_index(positions, lengths):
    prompt_ends = jnp.cumsum(lengths)
    prompt_starts = prompt_ends - lengths
    inside = (positions[:, None] >= prompt_starts[None, :]).astype(jnp.int32)
    segment = jnp.sum(inside, axis=1) - 1
    members = jnp.arange(lengths.shape[0], dtype=jnp.int32)[None, :] == segment[:, None]
    offset = positions - jnp.sum(jnp.where(members, prompt_starts[None, :], 0), axis=1)
    return (segment, offset, members)


def slot_lookup(adapter, adapter_slot):
    matches = jnp.arange(adapter_slot.shape[0], dtype=jnp.int32)[None, :] == adapter[:, None]
    return jnp.sum(jnp.where(matches, adapter_slot[None, :], 0), axis=1)


def rotate(vectors, offset):
    half_dim = vectors.shape[-1] // 2
    frequency = jnp.exp(
        jnp.arange(half_dim, dtype=jnp.float32) * (-2.0 * math.log(THETA) / vectors.shape[-1])
    )
    angles = offset.astype(jnp.float32)[:, None] * frequency[None, :]
    cosine = jnp.cos(angles)[:, None, :]
    sine_table = jnp.sin(angles)[:, None, :]
    first_half = vectors[..., :half_dim]
    second_half = vectors[..., half_dim:]
    return jnp.concatenate(
        [
            first_half * cosine - second_half * sine_table,
            second_half * cosine + first_half * sine_table,
        ],
        axis=-1,
    )


def adapter_terms(row_block, code_rows, a_in, pieces):
    table_count, rank_cols, in_width = a_in.shape
    projected = lax.dot_general(
        row_block,
        a_in.reshape(table_count * rank_cols, in_width),
        (((1,), (1,)), ((), ())),
        preferred_element_type=jnp.float32,
    )
    chosen = (jnp.arange(table_count, dtype=jnp.int32)[None, :] == code_rows[:, None]).astype(
        jnp.float32
    )
    low_rank = (projected.reshape(-1, table_count, rank_cols) * chosen[:, :, None]).astype(
        jnp.bfloat16
    )
    results = []
    for col_start, b_table in pieces:
        width_rank = b_table.shape[1]
        section = low_rank[:, :, col_start : col_start + width_rank].reshape(
            -1, table_count * width_rank
        )
        results.append(
            jnp.dot(
                section,
                b_table.reshape(table_count * width_rank, b_table.shape[2]),
                preferred_element_type=jnp.float32,
            ).astype(jnp.bfloat16)
        )
    return tuple(results)


def on_device(
    tokens,
    norm_gain,
    w_query,
    w_key,
    w_value,
    w_output,
    qkv_in,
    q_out,
    kv_out,
    o_in,
    o_out,
    lengths,
    prompt_adapter,
    adapter_slot,
):
    tok_rows = tokens.shape[0]
    tok_count = lax.axis_size("tok")
    own_count = lax.axis_size("own")
    per_owner = qkv_in.shape[0]
    device_here = lax.axis_index(("tok", "own"))
    positions = device_here * tok_rows + jnp.arange(tok_rows, dtype=jnp.int32)
    segment, offset, members = prompt_index(positions, lengths)
    prompt_count = lengths.shape[0]
    first_segment = segment[0]
    code_rows = segment - first_segment
    normed = rms_norm(tokens, norm_gain)
    tables = (qkv_in, q_out, kv_out, o_in, o_out)
    table_shapes = tuple((table.shape[1:] for table in tables))
    packed = jnp.concatenate([table.reshape(per_owner, -1) for table in tables], axis=1)
    all_slots = lax.all_gather(packed, "own", axis=0, tiled=True)
    own_here = lax.axis_index("own")
    group_blocks = jnp.arange(tok_count, dtype=jnp.int32) * own_count + own_here
    prompt_starts = jnp.cumsum(lengths) - lengths
    group_first = (
        jnp.sum(
            (group_blocks[:, None] * tok_rows >= prompt_starts[None, :]).astype(jnp.int32), axis=1
        )
        - 1
    )
    group_segments = jnp.minimum(
        group_first[:, None] + jnp.arange(SEG_DEV, dtype=jnp.int32)[None, :], prompt_count - 1
    )
    group_slots = jnp.take(adapter_slot, jnp.take(prompt_adapter, group_segments))
    outgoing = jnp.take(all_slots, group_slots.reshape(-1), axis=0).reshape(
        tok_count, SEG_DEV, packed.shape[1]
    )
    incoming = lax.all_to_all(outgoing, "tok", 0, 0, tiled=True)
    selected = []
    col = 0
    for table_shape in table_shapes:
        width = table_shape[0] * table_shape[1]
        piece = incoming[:, :, col : col + width].reshape(
            tok_count, SEG_DEV, table_shape[0], table_shape[1]
        )
        col += width
        selected.append(
            jnp.transpose(piece, (1, 2, 0, 3)).reshape(
                SEG_DEV, table_shape[0], tok_count * table_shape[1]
            )
        )
    input_maps, query_maps, keyvalue_maps, output_in_maps, output_out_maps = selected
    delta_q, delta_k, delta_v = adapter_terms(
        normed,
        code_rows,
        input_maps,
        ((0, query_maps), (RANK, keyvalue_maps[:, :RANK]), (2 * RANK, keyvalue_maps[:, RANK:])),
    )
    base_q = jnp.dot(normed, w_query, preferred_element_type=jnp.float32)
    base_k = jnp.dot(normed, w_key, preferred_element_type=jnp.float32)
    base_v = jnp.dot(normed, w_value, preferred_element_type=jnp.float32)
    query_lin = (base_q + delta_q.astype(jnp.float32)).reshape(tok_rows, HEADS, HEAD_WIDTH)
    queries = rotate(query_lin, offset).reshape(tok_rows, D).astype(jnp.bfloat16)
    key_lin = (base_k + delta_k.astype(jnp.float32)).reshape(tok_rows, KV_HEADS, HEAD_WIDTH)
    key_rows = rotate(key_lin, offset).reshape(tok_rows, KVW).astype(jnp.bfloat16)
    value_rows = (base_v + delta_v.astype(jnp.float32)).astype(jnp.bfloat16)
    key_value = jnp.concatenate([key_rows, value_rows], axis=1)
    key_store = jnp.zeros(((REACH + 1) * tok_rows, 2 * KVW), jnp.bfloat16)
    key_store = lax.dynamic_update_slice_in_dim(key_store, key_value, REACH * tok_rows, 0)
    window = key_store
    moving = key_value
    for turn_index in range(REACH):
        moving = from_behind(moving, ("tok", "own"), 1)
        window = lax.dynamic_update_slice_in_dim(
            window, moving, (REACH - 1 - turn_index) * tok_rows, 0
        )
    key_positions = (
        device_here * tok_rows
        - REACH * tok_rows
        + jnp.arange((REACH + 1) * tok_rows, dtype=jnp.int32)
    )
    key_segment = prompt_index(key_positions, lengths)[0]
    allowed = (segment[:, None] == key_segment[None, :]) & (
        key_positions[None, :] <= positions[:, None]
    )
    groups = HEADS // KV_HEADS
    key_count = window.shape[0]
    query_head_rows = queries.reshape(tok_rows, KV_HEADS, groups, HEAD_WIDTH)
    key_head_rows = window[:, :KVW].reshape(key_count, KV_HEADS, HEAD_WIDTH)
    value_head_rows = window[:, KVW:].reshape(key_count, KV_HEADS, HEAD_WIDTH)
    score_matrix = jnp.einsum(
        "qkzr,ckr->kzqc", query_head_rows, key_head_rows, preferred_element_type=jnp.float32
    ) * HEAD_WIDTH ** (-0.5)
    score_matrix = jnp.where(allowed[None, None], score_matrix, -1e30)
    top_score = jnp.max(score_matrix, axis=-1, keepdims=True)
    exp_scores = jnp.exp(score_matrix - top_score)
    row_total = jnp.sum(exp_scores, axis=-1)
    rounded_values = exp_scores.astype(jnp.bfloat16)
    summed_rows = jnp.einsum(
        "iyxv,vip->xiyp", rounded_values, value_head_rows, preferred_element_type=jnp.float32
    )
    attn_rows = (
        (summed_rows / jnp.transpose(row_total, (2, 0, 1))[..., None])
        .reshape(tok_rows, D)
        .astype(jnp.bfloat16)
    )
    delta_o = adapter_terms(attn_rows, code_rows, output_in_maps, ((0, output_out_maps),))[0]
    projected_out = jnp.dot(
        attn_rows, w_output, preferred_element_type=jnp.float32
    ) + delta_o.astype(jnp.float32)
    mixed_rows = (tokens.astype(jnp.float32) + projected_out).astype(jnp.bfloat16)
    return (mixed_rows, key_value)


def solution(mesh):
    return jax.shard_map(
        on_device,
        mesh=mesh,
        in_specs=(
            P(("tok", "own"), None),
            P(),
            P(),
            P(),
            P(),
            P(),
            P("own", None, "tok"),
            P("own", None, "tok"),
            P("own", None, "tok"),
            P("own", None, "tok"),
            P("own", None, "tok"),
            P(),
            P(),
            P(),
        ),
        out_specs=(P(("tok", "own"), None), P(("tok", "own"), None)),
        check_vma=False,
    )
```

profile of v0, /device:TPU:24, one launch (start us, length us, event | category | flops | bytes accessed | tf_op | source)
XLA Modules:
  0.0 273.8 jit_solution(17576496565474559692)
XLA Ops:
  9.0 15.0 %all_gather.3 = bf16[64,7680]{1,0:T(8,128)(2,1)} all-gather(bf16[8,7680]{1,0:T(8,128)(2,1)S(1)} %constant_dynamic-update-slice_fusion), channel_id=1, replica_groups=mesh['tok'=16,'own'=8] {'own'}, dimensions={0}, use_global_device_ids=true | all-gather | bytes 1105920 | tf_op jit(solution)/shard_map/all_gather | solution.py:125
  24.0 4.8 %gather_fusion = bf16[80,7680]{1,0:T(8,128)(2,1)} fusion(bf16[64,7680]{1,0:T(8,128)(2,1)} %all_gather.3, s32[1024]{0:T(1024)S(1)} %pad_clamp_fusion), kind=kCustom, calls=%fused_computation.2 | custom fusion | bytes 2457920 | tf_op jit(solution)/shard_map/jit(_take)/gather | solution.py:139
  28.8 2.6 gather.10
  31.5 3.1 %broadcast_select_fusion = bf16[16,5,7680]{2,1,0:T(8,128)(2,1)} fusion(bf16[16,5,7680]{2,1,0:T(8,128)(2,1)} %gather.10, pred[16,5]{1,0:T(8,128)(4,1)S(1)} %get-tuple-element.3), kind=kLoop, calls=%fused_computation.18 | loop fusion | flops 614400 | bytes 2457680 | tf_op jit(solution)/shard_map/jit(_take)/select_n | solution.py:139
  34.6 8.3 %all-to-all-start = ((bf16[16,5,7680]{2,1,0:T(8,128)(2,1)}), bf16[16,5,7680]{2,1,0:T(8,128)(2,1)}, u32[]{:S(2)}, u32[]{:S(2)}) async-start(bf16[16,5,7680]{2,1,0:T(8,128)(2,1)} %broadcast_select_fusion), calls=%async_computation | async-start | bytes 3932160 | tf_op jit(solution)/shard_map/all_to_all | solution.py:142
  44.9 25.3 %all-to-all-done = bf16[16,5,7680]{2,1,0:T(8,128)(2,1)} async-done(((bf16[16,5,7680]{2,1,0:T(8,128)(2,1)}), bf16[16,5,7680]{2,1,0:T(8,128)(2,1)}, u32[]{:S(2)}, u32[]{:S(2)}) %all-to-all-start) | async-done | bytes 1228832 | tf_op jit(solution)/shard_map/all_to_all | solution.py:142
  71.2 1.9 reshape.334
  73.0 2.2 copy.47
  75.2 2.3 reshape.335
  78.9 2.7 reshape.333
  81.5 2.4 copy.45
  84.0 2.2 dot_general.41
  93.0 1.9 collective-permute-start
  95.0 9.3 %collective-permute-done = bf16[128,768]{1,0:T(8,128)(2,1)S(1)} collective-permute-done((bf16[128,768]{1,0:T(8,128)(2,1)S(1)}, bf16[128,768]{1,0:T(8,128)(2,1)S(1)}, u32[]{:S(2)}, u32[]{:S(2)}) %collective-permute-start) | collective-permute-done | bytes 196640 | tf_op jit(solution)/shard_map/ppermute | solution.py:22
  104.2 2.1 collective-permute-start.1
  107.4 8.1 %collective-permute-done.1 = bf16[128,768]{1,0:T(8,128)(2,1)} collective-permute-done((bf16[128,768]{1,0:T(8,128)(2,1)S(1)}, bf16[128,768]{1,0:T(8,128)(2,1)}, u32[]{:S(2)}, u32[]{:S(2)}) %collective-permute-start.1) | collective-permute-done | bytes 196640 | tf_op jit(solution)/shard_map/ppermute | solution.py:22
  115.5 1.9 collective-permute-start.2
  117.5 2.0 fusion.43
  123.8 2.0 reshape_reshape.9
  125.8 1.7 copy.56
  129.8 2.0 dot_general.51
  131.7 1.7 copy.52
  137.0 1.9 collective-permute-start.3
  139.9 8.5 %collective-permute-done.3 = bf16[128,768]{1,0:T(8,128)(2,1)S(1)} collective-permute-done((bf16[128,768]{1,0:T(8,128)(2,1)}, bf16[128,768]{1,0:T(8,128)(2,1)S(1)}, u32[]{:S(2)}, u32[]{:S(2)}) %collective-permute-start.3) | collective-permute-done | bytes 196640 | tf_op jit(solution)/shard_map/ppermute | solution.py:22
  148.4 1.9 collective-permute-start.4
  150.3 2.2 convolution_add_fusion.1
  152.5 2.1 copy.54
  154.9 4.8 %collective-permute-done.4 = bf16[128,768]{1,0:T(8,128)(2,1)} collective-permute-done((bf16[128,768]{1,0:T(8,128)(2,1)S(1)}, bf16[128,768]{1,0:T(8,128)(2,1)}, u32[]{:S(2)}, u32[]{:S(2)}) %collective-permute-start.4) | collective-permute-done | bytes 196640 | tf_op jit(solution)/shard_map/ppermute | solution.py:22
  159.7 1.9 collective-permute-start.5
  161.8 9.4 %collective-permute-done.5 = bf16[128,768]{1,0:T(8,128)(2,1)S(1)} collective-permute-done((bf16[128,768]{1,0:T(8,128)(2,1)}, bf16[128,768]{1,0:T(8,128)(2,1)S(1)}, u32[]{:S(2)}, u32[]{:S(2)}) %collective-permute-start.5) | collective-permute-done | bytes 196640 | tf_op jit(solution)/shard_map/ppermute | solution.py:22
  171.1 1.9 collective-permute-start.6
  173.1 9.2 %collective-permute-done.6 = bf16[128,768]{1,0:T(8,128)(2,1)S(1)} collective-permute-done((bf16[128,768]{1,0:T(8,128)(2,1)S(1)}, bf16[128,768]{1,0:T(8,128)(2,1)S(1)}, u32[]{:S(2)}, u32[]{:S(2)}) %collective-permute-start.6) | collective-permute-done | bytes 196640 | tf_op jit(solution)/shard_map/ppermute | solution.py:22
  182.3 1.9 collective-permute-start.7
  186.1 7.4 %collective-permute-done.7 = bf16[128,768]{1,0:T(8,128)(2,1)S(1)} collective-permute-done((bf16[128,768]{1,0:T(8,128)(2,1)S(1)}, bf16[128,768]{1,0:T(8,128)(2,1)S(1)}, u32[]{:S(2)}, u32[]{:S(2)}) %collective-permute-start.7) | collective-permute-done | bytes 196640 | tf_op jit(solution)/shard_map/ppermute | solution.py:22
  193.5 1.9 collective-permute-start.8
  196.4 8.3 %collective-permute-done.8 = bf16[128,768]{1,0:T(8,128)(2,1)S(1)} collective-permute-done((bf16[128,768]{1,0:T(8,128)(2,1)S(1)}, bf16[128,768]{1,0:T(8,128)(2,1)S(1)}, u32[]{:S(2)}, u32[]{:S(2)}) %collective-permute-start.8) | collective-permute-done | bytes 196640 | tf_op jit(solution)/shard_map/ppermute | solution.py:22
  204.7 1.9 collective-permute-start.9
  206.7 9.2 %collective-permute-done.9 = bf16[128,768]{1,0:T(8,128)(2,1)S(1)} collective-permute-done((bf16[128,768]{1,0:T(8,128)(2,1)S(1)}, bf16[128,768]{1,0:T(8,128)(2,1)S(1)}, u32[]{:S(2)}, u32[]{:S(2)}) %collective-permute-start.9) | collective-permute-done | bytes 196640 | tf_op jit(solution)/shard_map/ppermute | solution.py:22
  215.9 1.9 collective-permute-start.10
  217.9 9.2 %collective-permute-done.10 = bf16[128,768]{1,0:T(8,128)(2,1)S(1)} collective-permute-done((bf16[128,768]{1,0:T(8,128)(2,1)S(1)}, bf16[128,768]{1,0:T(8,128)(2,1)S(1)}, u32[]{:S(2)}, u32[]{:S(2)}) %collective-permute-start.10) | collective-permute-done | bytes 196640 | tf_op jit(solution)/shard_map/ppermute | solution.py:22
  227.1 1.9 collective-permute-start.11
  229.1 9.2 %collective-permute-done.11 = bf16[128,768]{1,0:T(8,128)(2,1)S(1)} collective-permute-done((bf16[128,768]{1,0:T(8,128)(2,1)S(1)}, bf16[128,768]{1,0:T(8,128)(2,1)S(1)}, u32[]{:S(2)}, u32[]{:S(2)}) %collective-permute-start.11) | collective-permute-done | bytes 196640 | tf_op jit(solution)/shard_map/ppermute | solution.py:22
  238.3 1.7 fusion.42
  240.1 2.5 copy.51
  242.6 2.5 copy.50
  245.1 9.0 %fusion.2 = (f32[6,3,128]{2,1,0:T(4,128)S(1)}, f32[6,1664,128,3]{2,1,3,0:T(8,128)}) fusion(pred[128,1664]{0,1:T(8,128)(4,1)S(1)} %compare_and_fusion, bf16[1664,6,64,1]{0,2,3,1:T(8,128)(2,1)} %bitcast.101, bf16[128,6,3,64]{0,3,2,1:T(8,128)(2,1)S(1)} %bitcast.105), kind=kOutput, calls=%fused_computation.7 | convolution fusion | flops 502232832 | bytes 17130496 | tf_op jit(solution)/shard_map/qkzr,ckr->kzqc/dot_general | solution.py:195
  254.0 8.6 %fusion = f32[6,3,128]{2,1,0:T(4,128)S(1)} fusion(f32[6,1664,128,3]{2,1,3,0:T(8,128)} %get-tuple-element.17, f32[6,3,128]{2,1,0:T(4,128)S(1)} %get-tuple-element.16, pred[128,1664]{0,1:T(8,128)(4,1)S(1)} %compare_and_fusion), kind=kLoop, calls=%fused_computation.5 | loop fusion | flops 15333120 | bytes 15566848 | tf_op jit(solution)/shard_map/reduce_sum | solution.py:201
  262.7 9.2 %fusion.23 = bf16[128,6,3,64]{0,3,2,1:T(8,128)(2,1)S(1)} fusion(bf16[1664,6,64,1]{0,2,3,1:T(8,128)(2,1)S(1)} %bitcast.109, f32[6,1664,128,3]{2,1,3,0:T(8,128)} %get-tuple-element.17, f32[6,3,128]{2,1,0:T(4,128)S(1)} %get-tuple-element.16, pred[128,1664]{0,1:T(8,128)(4,1)S(1)} %compare_and_fusion, f32[128,6,3]{0,2,1:T(4,128)S(1)} %bitcast.116), kind=kOutput, calls=%fused_computation.34 | convolution fusion | flops 506363904 | bytes 17139712 | tf_op jit(solution)/shard_map/iyxv,vip->xiyp/dot_general | solution.py:203
  (157 shorter events, 36.4 us)
Async XLA Ops:
  0.6 149.7 %copy-start = (bf16[1152,1152]{1,0:T(8,128)(2,1)S(1)}, bf16[1152,1152]{1,0:T(8,128)(2,1)}, u32[]{:S(2)}) copy-start(bf16[1152,1152]{1,0:T(8,128)(2,1)} %param.18) | copy-start | bytes 7962628
  0.6 4.8 %copy-start.1 = (s32[64]{0:T(128)S(1)}, s32[64]{0:T(128)}, u32[]{:S(2)}) copy-start(s32[64]{0:T(128)} %param.28) | copy-start | bytes 772
  5.4 1.5 copy-start.2
  7.0 1.6 copy-start.19
  7.0 1.7 copy-start.23
  34.6 8.3 %copy-start.3 = (bf16[128,1152]{1,0:T(8,128)(2,1)S(1)}, bf16[128,1152]{1,0:T(8,128)(2,1)}, u32[]{:S(2)}) copy-start(bf16[128,1152]{1,0:T(8,128)(2,1)} %param.16) | copy-start | bytes 884740
  34.6 9.4 %copy-start.26 = (bf16[1152]{0:T(1024)(128)(2,1)S(1)}, bf16[1152]{0:T(1024)(128)(2,1)}, u32[]{:S(2)}) copy-start(bf16[1152]{0:T(1024)(128)(2,1)} %param.17) | copy-start | bytes 6916
  34.6 35.6 %all-to-all-start = ((bf16[16,5,7680]{2,1,0:T(8,128)(2,1)}), bf16[16,5,7680]{2,1,0:T(8,128)(2,1)}, u32[]{:S(2)}, u32[]{:S(2)}) async-start(bf16[16,5,7680]{2,1,0:T(8,128)(2,1)} %broadcast_select_fusion), calls=%async_computation | async-start | bytes 3932160 | tf_op jit(solution)/shard_map/all_to_all | solution.py:142
  42.9 27.3 %copy-start.29 = (s32[128]{0:T(128)}, s32[128]{0:T(128)S(1)}, u32[]{:S(2)}) copy-start(s32[128]{0:T(128)S(1)} %iota_add_fusion.1) | copy-start | bytes 1540
  43.1 1.0 copy-start.20
  43.2 27.0 %copy-start.31 = (s32[128]{0:T(128)}, s32[128]{0:T(128)S(1)}, u32[]{:S(2)}) copy-start(s32[128]{0:T(128)S(1)} %broadcast_add_fusion.1) | copy-start | bytes 1540
  44.0 42.1 %copy-start.18 = (f32[1152]{0:T(1024)}, f32[1152]{0:T(1024)S(1)}, u32[]{:S(2)}) copy-start(f32[1152]{0:T(1024)S(1)} %convert_element_type.91) | copy-start | bytes 13828
  44.1 42.1 %copy-start.25 = (f32[128]{0:T(128)}, f32[128]{0:T(128)S(1)}, u32[]{:S(2)}) copy-start(f32[128]{0:T(128)S(1)} %add_rsqrt_fusion) | copy-start | bytes 1540
  44.1 42.0 %copy-start.27 = (f32[128,5]{0,1:T(8,128)}, f32[128,5]{0,1:T(8,128)S(1)}, u32[]{:S(2)}) copy-start(f32[128,5]{0,1:T(8,128)S(1)} %fusion.34) | copy-start | bytes 7684
  44.9 45.6 %copy-start.15 = (f32[128,32]{0,1:T(8,128)}, f32[128,32]{0,1:T(8,128)S(1)}, u32[]{:S(2)}) copy-start(f32[128,32]{0,1:T(8,128)S(1)} %get-tuple-element.14) | copy-start | bytes 49156
  86.6 2.1 copy-start.22
  90.5 4.5 %copy-start.24 = (s32[1664]{0:T(1024)S(1)}, s32[1664]{0:T(1024)}, u32[]{:S(2)}) copy-start(s32[1664]{0:T(1024)} %convert_reduce_fusion) | copy-start | bytes 19972
  90.5 15.9 %copy-start.21 = (s32[1664]{0:T(1024)S(1)}, s32[1664]{0:T(1024)}, u32[]{:S(2)}) copy-start(s32[1664]{0:T(1024)} %copy-done.20) | copy-start | bytes 19972
  90.5 15.9 %copy-start.30 = (s32[128]{0:T(128)S(1)}, s32[128]{0:T(128)}, u32[]{:S(2)}) copy-start(s32[128]{0:T(128)} %copy-done.29) | copy-start | bytes 1540
  90.5 15.9 %copy-start.32 = (s32[128]{0:T(128)S(1)}, s32[128]{0:T(128)}, u32[]{:S(2)}) copy-start(s32[128]{0:T(128)} %copy-done.31) | copy-start | bytes 1540
  93.0 22.5 %copy-start.7 = (bf16[128,768]{1,0:T(8,128)(2,1)}, bf16[128,768]{1,0:T(8,128)(2,1)S(1)}, u32[]{:S(2)}) copy-start(bf16[128,768]{1,0:T(8,128)(2,1)S(1)} %pad_maximum_fusion.1) | copy-start | bytes 589828
  93.0 11.2 %collective-permute-start = (bf16[128,768]{1,0:T(8,128)(2,1)S(1)}, bf16[128,768]{1,0:T(8,128)(2,1)S(1)}, u32[]{:S(2)}, u32[]{:S(2)}) collective-permute-start(bf16[128,768]{1,0:T(8,128)(2,1)S(1)} %pad_maximum_fusion.1), channel_id=1, source_target_pairs={{0,1},{1,2},{2,3},{3,4},{4,5},{5,6},{6,7},{7,8},{8,9},{9,10},{10,1... | collective-permute-start | bytes 589832 | tf_op jit(solution)/shard_map/ppermute | solution.py:22
  104.2 11.3 %copy-start.10 = (bf16[128,768]{1,0:T(8,128)(2,1)}, bf16[128,768]{1,0:T(8,128)(2,1)S(1)}, u32[]{:S(2)}) copy-start(bf16[128,768]{1,0:T(8,128)(2,1)S(1)} %collective-permute-done) | copy-start | bytes 589828
  104.2 11.3 %collective-permute-start.1 = (bf16[128,768]{1,0:T(8,128)(2,1)S(1)}, bf16[128,768]{1,0:T(8,128)(2,1)}, u32[]{:S(2)}, u32[]{:S(2)}) collective-permute-start(bf16[128,768]{1,0:T(8,128)(2,1)S(1)} %collective-permute-done), channel_id=1, source_target_pairs={{0,1},{1,2},{2,3},{3,4},{4,5},{5,6},{6,7},{7,8},{8,9},{9,10},{10,1... | collective-permute-start | bytes 589832 | tf_op jit(solution)/shard_map/ppermute | solution.py:22
  115.5 21.4 %collective-permute-start.2 = (bf16[128,768]{1,0:T(8,128)(2,1)}, bf16[128,768]{1,0:T(8,128)(2,1)}, u32[]{:S(2)}, u32[]{:S(2)}) collective-permute-start(bf16[128,768]{1,0:T(8,128)(2,1)} %collective-permute-done.1), channel_id=1, source_target_pairs={{0,1},{1,2},{2,3},{3,4},{4,5},{5,6},{6,7},{7,8},{8,9},{9,10},{10,1... | collective-permute-start | bytes 589832 | tf_op jit(solution)/shard_map/ppermute | solution.py:22
  137.0 11.4 %collective-permute-start.3 = (bf16[128,768]{1,0:T(8,128)(2,1)}, bf16[128,768]{1,0:T(8,128)(2,1)S(1)}, u32[]{:S(2)}, u32[]{:S(2)}) collective-permute-start(bf16[128,768]{1,0:T(8,128)(2,1)} %collective-permute-done.2), channel_id=1, source_target_pairs={{0,1},{1,2},{2,3},{3,4},{4,5},{5,6},{6,7},{7,8},{8,9},{9,10},{10,1... | collective-permute-start | bytes 589832 | tf_op jit(solution)/shard_map/ppermute | solution.py:22
  139.9 14.8 %copy-start.8 = (bf16[128,768]{1,0:T(8,128)(2,1)S(1)}, bf16[128,768]{1,0:T(8,128)(2,1)}, u32[]{:S(2)}) copy-start(bf16[128,768]{1,0:T(8,128)(2,1)} %copy-done.7) | copy-start | bytes 589828
  148.4 6.2 %copy-start.12 = (bf16[128,768]{1,0:T(8,128)(2,1)}, bf16[128,768]{1,0:T(8,128)(2,1)S(1)}, u32[]{:S(2)}) copy-start(bf16[128,768]{1,0:T(8,128)(2,1)S(1)} %collective-permute-done.3) | copy-start | bytes 589828
  148.4 11.3 %collective-permute-start.4 = (bf16[128,768]{1,0:T(8,128)(2,1)S(1)}, bf16[128,768]{1,0:T(8,128)(2,1)}, u32[]{:S(2)}, u32[]{:S(2)}) collective-permute-start(bf16[128,768]{1,0:T(8,128)(2,1)S(1)} %collective-permute-done.3), channel_id=1, source_target_pairs={{0,1},{1,2},{2,3},{3,4},{4,5},{5,6},{6,7},{7,8},{8,9},{9,10},{10,1... | collective-permute-start | bytes 589832 | tf_op jit(solution)/shard_map/ppermute | solution.py:22
  154.7 7.0 %copy-start.5 = (f32[128,1152]{0,1:T(8,128)S(1)}, f32[128,1152]{0,1:T(8,128)}, u32[]{:S(2)}) copy-start(f32[128,1152]{0,1:T(8,128)} %copy.54) | copy-start | bytes 1769476
  154.7 7.0 %copy-start.16 = (f32[128,32]{0,1:T(8,128)S(1)}, f32[128,32]{0,1:T(8,128)}, u32[]{:S(2)}) copy-start(f32[128,32]{0,1:T(8,128)} %copy-done.15) | copy-start | bytes 49156
  154.7 7.0 %copy-start.17 = (f32[128,32]{0,1:T(8,128)S(1)}, f32[128,32]{0,1:T(8,128)}, u32[]{:S(2)}) copy-start(f32[128,32]{0,1:T(8,128)} %get-tuple-element.15) | copy-start | bytes 49156
  154.7 18.4 %copy-start.11 = (bf16[128,768]{1,0:T(8,128)(2,1)S(1)}, bf16[128,768]{1,0:T(8,128)(2,1)}, u32[]{:S(2)}) copy-start(bf16[128,768]{1,0:T(8,128)(2,1)} %copy-done.10) | copy-start | bytes 589828
  154.9 40.6 %copy-start.13 = (bf16[128,768]{1,0:T(8,128)(2,1)S(1)}, bf16[128,768]{1,0:T(8,128)(2,1)}, u32[]{:S(2)}) copy-start(bf16[128,768]{1,0:T(8,128)(2,1)} %copy-done.12) | copy-start | bytes 589828
  159.7 11.4 %collective-permute-start.5 = (bf16[128,768]{1,0:T(8,128)(2,1)}, bf16[128,768]{1,0:T(8,128)(2,1)S(1)}, u32[]{:S(2)}, u32[]{:S(2)}) collective-permute-start(bf16[128,768]{1,0:T(8,128)(2,1)} %collective-permute-done.4), channel_id=1, source_target_pairs={{0,1},{1,2},{2,3},{3,4},{4,5},{5,6},{6,7},{7,8},{8,9},{9,10},{10,1... | collective-permute-start | bytes 589832 | tf_op jit(solution)/shard_map/ppermute | solution.py:22
  171.1 11.2 %collective-permute-start.6 = (bf16[128,768]{1,0:T(8,128)(2,1)S(1)}, bf16[128,768]{1,0:T(8,128)(2,1)S(1)}, u32[]{:S(2)}, u32[]{:S(2)}) collective-permute-start(bf16[128,768]{1,0:T(8,128)(2,1)S(1)} %collective-permute-done.5), channel_id=1, source_target_pairs={{0,1},{1,2},{2,3},{3,4},{4,5},{5,6},{6,7},{7,8},{8,9},{9,10},{10,1... | collective-permute-start | bytes 589832 | tf_op jit(solution)/shard_map/ppermute | solution.py:22
  182.3 11.2 %collective-permute-start.7 = (bf16[128,768]{1,0:T(8,128)(2,1)S(1)}, bf16[128,768]{1,0:T(8,128)(2,1)S(1)}, u32[]{:S(2)}, u32[]{:S(2)}) collective-permute-start(bf16[128,768]{1,0:T(8,128)(2,1)S(1)} %collective-permute-done.6), channel_id=1, source_target_pairs={{0,1},{1,2},{2,3},{3,4},{4,5},{5,6},{6,7},{7,8},{8,9},{9,10},{10,1... | collective-permute-start | bytes 589832 | tf_op jit(solution)/shard_map/ppermute | solution.py:22
  193.5 11.2 %collective-permute-start.8 = (bf16[128,768]{1,0:T(8,128)(2,1)S(1)}, bf16[128,768]{1,0:T(8,128)(2,1)S(1)}, u32[]{:S(2)}, u32[]{:S(2)}) collective-permute-start(bf16[128,768]{1,0:T(8,128)(2,1)S(1)} %collective-permute-done.7), channel_id=1, source_target_pairs={{0,1},{1,2},{2,3},{3,4},{4,5},{5,6},{6,7},{7,8},{8,9},{9,10},{10,1... | collective-permute-start | bytes 589832 | tf_op jit(solution)/shard_map/ppermute | solution.py:22
  204.7 11.2 %collective-permute-start.9 = (bf16[128,768]{1,0:T(8,128)(2,1)S(1)}, bf16[128,768]{1,0:T(8,128)(2,1)S(1)}, u32[]{:S(2)}, u32[]{:S(2)}) collective-permute-start(bf16[128,768]{1,0:T(8,128)(2,1)S(1)} %collective-permute-done.8), channel_id=1, source_target_pairs={{0,1},{1,2},{2,3},{3,4},{4,5},{5,6},{6,7},{7,8},{8,9},{9,10},{10,1... | collective-permute-start | bytes 589832 | tf_op jit(solution)/shard_map/ppermute | solution.py:22
  215.9 11.2 %collective-permute-start.10 = (bf16[128,768]{1,0:T(8,128)(2,1)S(1)}, bf16[128,768]{1,0:T(8,128)(2,1)S(1)}, u32[]{:S(2)}, u32[]{:S(2)}) collective-permute-start(bf16[128,768]{1,0:T(8,128)(2,1)S(1)} %collective-permute-done.9), channel_id=1, source_target_pairs={{0,1},{1,2},{2,3},{3,4},{4,5},{5,6},{6,7},{7,8},{8,9},{9,10},{10,1... | collective-permute-start | bytes 589832 | tf_op jit(solution)/shard_map/ppermute | solution.py:22
  227.1 11.2 %collective-permute-start.11 = (bf16[128,768]{1,0:T(8,128)(2,1)S(1)}, bf16[128,768]{1,0:T(8,128)(2,1)S(1)}, u32[]{:S(2)}, u32[]{:S(2)}) collective-permute-start(bf16[128,768]{1,0:T(8,128)(2,1)S(1)} %collective-permute-done.10), channel_id=1, source_target_pairs={{0,1},{1,2},{2,3},{3,4},{4,5},{5,6},{6,7},{7,8},{8,9},{9,10},{10,1... | collective-permute-start | bytes 589832 | tf_op jit(solution)/shard_map/ppermute | solution.py:22
  254.0 8.6 %copy-start.6 = (bf16[1664,384]{0,1:T(8,128)(2,1)S(1)}, bf16[1664,384]{0,1:T(8,128)(2,1)}, u32[]{:S(2)}) copy-start(bf16[1664,384]{0,1:T(8,128)(2,1)} %copy.50) | copy-start | bytes 3833860
  262.7 9.3 %copy-start.14 = (bf16[5,16,1152]{2,1,0:T(8,128)(2,1)S(1)}, bf16[5,16,1152]{2,1,0:T(8,128)(2,1)}, u32[]{:S(2)}) copy-start(bf16[5,16,1152]{2,1,0:T(8,128)(2,1)} %dot_general.51) | copy-start | bytes 552964
  262.7 9.3 %copy-start.28 = (f32[128,5]{0,1:T(8,128)S(1)}, f32[128,5]{0,1:T(8,128)}, u32[]{:S(2)}) copy-start(f32[128,5]{0,1:T(8,128)} %copy-done.27) | copy-start | bytes 7684
  262.7 9.5 %copy-start.9 = (bf16[80,1152]{1,0:T(8,128)(2,1)S(1)}, bf16[80,1152]{1,0:T(8,128)(2,1)}, u32[]{:S(2)}) copy-start(bf16[80,1152]{1,0:T(8,128)(2,1)} %reshape_reshape.9) | copy-start | bytes 552964
  262.7 9.7 %copy-start.4 = (bf16[1152,1152]{1,0:T(8,128)(2,1)S(1)}, bf16[1152,1152]{1,0:T(8,128)(2,1)}, u32[]{:S(2)}) copy-start(bf16[1152,1152]{1,0:T(8,128)(2,1)} %param.21) | copy-start | bytes 7962628
where the time goes:
time: 276 us; the launch traced here: 274 us
  waiting for transfers between devices  118 us (43%)
  local copies, waits for them, and re-layouts  62.1 us (22%)
  starting transfers between devices  31.4 us (11%)
  matrix products  28.8 us (10%)
  other arithmetic  16.9 us (6%)
  blocking collectives  15 us (5%)
    ppermute x12, waiting for transfers between devices, from_behind(): return lax.ppermute(block, axis, route)  92.7 us
    all_to_all x1, waiting for transfers between devices, on_device(): incoming = lax.all_to_all(outgoing, 'tok', 0, 0, tiled=True)  25.3 us
    ppermute x12, starting transfers between devices, from_behind(): return lax.ppermute(block, axis, route)  23.1 us
    all_gather x1, blocking collectives, on_device(): all_slots = lax.all_gather(packed, 'own', axis=0, tiled=True)  15 us
    dot_general x1, matrix products, on_device(): jnp.einsum('iyxv,vip->xiyp', rounded_values, value_head_rows, preferred_e...  9.21 us
    reshape x5, local copies, waits for them, and re-layouts, on_device(): incoming[:, :, col:col + width]  9 us
    dot_general x1, matrix products, on_device(): jnp.einsum('qkzr,ckr->kzqc', query_head_rows, key_head_rows, preferred_el...  8.99 us
    reduce_sum x1, other arithmetic, on_device(): row_total = jnp.sum(exp_scores, axis=-1)  8.61 us
  transfers between devices with their start and end apart: 13, of which 12 were waited for; matrix products, arithmetic and copies ran while one was open for 11% of the time, Pallas kernels for 0%

commit v1 on v0

--- a/solution.py
+++ b/solution.py
@@ -14,6 +14,14 @@
 SEG_DEV = 5
 EPS = 1e-05
 THETA = 10000.0
+
+
+def gather_by_exchange(shard, axis, dim):
+    size = lax.axis_size(axis)
+    repeats = [size if d == dim else 1 for d in range(shard.ndim)]
+    return lax.all_to_all(
+        jnp.tile(shard, repeats), axis, split_axis=dim, concat_axis=dim, tiled=True
+    )
 
 
 def from_behind(block, axis, distance):
@@ -122,7 +130,7 @@
     tables = (qkv_in, q_out, kv_out, o_in, o_out)
     table_shapes = tuple((table.shape[1:] for table in tables))
     packed = jnp.concatenate([table.reshape(per_owner, -1) for table in tables], axis=1)
-    all_slots = lax.all_gather(packed, "own", axis=0, tiled=True)
+    all_slots = gather_by_exchange(packed, "own", 0)
     own_here = lax.axis_index("own")
     group_blocks = jnp.arange(tok_count, dtype=jnp.int32) * own_count + own_here
     prompt_starts = jnp.cumsum(lengths) - lengths

time: 276 us -> 277 us (level)
  blocking collectives: 15 us -> 0 us
  waiting for transfers between devices: 118 us -> 128 us
  starting transfers between devices: 31.4 us -> 35.7 us
    all_gather x1 -> x0, blocking collectives: 15 us -> none  [on_device(): all_slots = lax.all_gather(packed, 'own', axis=0, tiled=True)]
    all_to_all x0 -> x1, waiting for transfers between devices: none -> 10 us  [gather_by_exchange(): lax.all_to_all(jnp.tile(shard, repeats), axis, split_axis=dim, concat_axi...]
    all_to_all x0 -> x1, starting transfers between devices: none -> 4.3 us  [gather_by_exchange(): lax.all_to_all(jnp.tile(shard, repeats), axis, split_axis=dim, concat_axi...]
  transfers between devices with their start and end apart: 13 -> 14, of which waited for: 12 -> 13; matrix products, arithmetic and copies ran while one was open for 11% -> 13% of each run, Pallas kernels for 0% -> 0%
where the time goes in v1:
time: 277 us; the launch traced here: 275 us
  waiting for transfers between devices  128 us (46%)
  local copies, waits for them, and re-layouts  64.6 us (23%)
  starting transfers between devices  35.7 us (13%)
  matrix products  28.8 us (10%)
  other arithmetic  16.2 us (6%)
    ppermute x12, waiting for transfers between devices, from_behind(): return lax.ppermute(block, axis, route)  92.9 us
    all_to_all x1, waiting for transfers between devices, on_device(): incoming = lax.all_to_all(outgoing, 'tok', 0, 0, tiled=True)  25.1 us
    ppermute x12, starting transfers between devices, from_behind(): return lax.ppermute(block, axis, route)  23.1 us
    all_to_all x1, waiting for transfers between devices, gather_by_exchange(): lax.all_to_all(jnp.tile(shard, repeats), axis, split_axis=dim, concat_axi...  10 us
    dot_general x1, matrix products, on_device(): jnp.einsum('iyxv,vip->xiyp', rounded_values, value_head_rows, preferred_e...  9.21 us
    reshape x5, local copies, waits for them, and re-layouts, on_device(): incoming[:, :, col:col + width]  9 us
    dot_general x1, matrix products, on_device(): jnp.einsum('qkzr,ckr->kzqc', query_head_rows, key_head_rows, preferred_el...  8.99 us
    reduce_sum x1, other arithmetic, on_device(): row_total = jnp.sum(exp_scores, axis=-1)  8.61 us
  transfers between devices with their start and end apart: 14, of which 13 were waited for; matrix products, arithmetic and copies ran while one was open for 13% of the time, Pallas kernels for 0%

profile of v1, /device:TPU:24, one launch (start us, length us, event | category | flops | bytes accessed | tf_op | source)
XLA Modules:
  0.0 274.9 jit_solution(5658722360890389971)
XLA Ops:
  6.6 4.3 %all-to-all-start = ((bf16[8,8,7680]{2,1,0:T(8,128)(2,1)}), bf16[8,8,7680]{2,1,0:T(8,128)(2,1)}, u32[]{:S(2)}, u32[]{:S(2)}) async-start(bf16[8,8,7680]{2,1,0:T(8,128)(2,1)} %tile.2), calls=%async_computation | async-start | bytes 1966080 | tf_op jit(solution)/shard_map/all_to_all | solution.py:22
  16.2 10.0 %all-to-all-done = bf16[8,8,7680]{2,1,0:T(8,128)(2,1)} async-done(((bf16[8,8,7680]{2,1,0:T(8,128)(2,1)}), bf16[8,8,7680]{2,1,0:T(8,128)(2,1)}, u32[]{:S(2)}, u32[]{:S(2)}) %all-to-all-start) | async-done | bytes 983072 | tf_op jit(solution)/shard_map/all_to_all | solution.py:22
  26.2 4.8 %gather_fusion = bf16[80,7680]{1,0:T(8,128)(2,1)} fusion(bf16[64,7680]{1,0:T(8,128)(2,1)} %bitcast.2, s32[1024]{0:T(1024)S(1)} %pad_clamp_fusion), kind=kCustom, calls=%fused_computation.2 | custom fusion | bytes 2457920 | tf_op jit(solution)/shard_map/jit(_take)/gather | solution.py:147
  31.1 2.6 gather.10
  33.7 3.1 %broadcast_select_fusion = bf16[16,5,7680]{2,1,0:T(8,128)(2,1)} fusion(bf16[16,5,7680]{2,1,0:T(8,128)(2,1)} %gather.10, pred[16,5]{1,0:T(8,128)(4,1)S(1)} %get-tuple-element.3), kind=kLoop, calls=%fused_computation.18 | loop fusion | flops 614400 | bytes 2457680 | tf_op jit(solution)/shard_map/jit(_take)/select_n | solution.py:147
  36.8 8.3 %all-to-all-start.1 = ((bf16[16,5,7680]{2,1,0:T(8,128)(2,1)}), bf16[16,5,7680]{2,1,0:T(8,128)(2,1)}, u32[]{:S(2)}, u32[]{:S(2)}) async-start(bf16[16,5,7680]{2,1,0:T(8,128)(2,1)} %broadcast_select_fusion), calls=%async_computation.1 | async-start | bytes 3932160 | tf_op jit(solution)/shard_map/all_to_all | solution.py:150
  46.0 25.1 %all-to-all-done.1 = bf16[16,5,7680]{2,1,0:T(8,128)(2,1)} async-done(((bf16[16,5,7680]{2,1,0:T(8,128)(2,1)}), bf16[16,5,7680]{2,1,0:T(8,128)(2,1)}, u32[]{:S(2)}, u32[]{:S(2)}) %all-to-all-start.1) | async-done | bytes 1228832 | tf_op jit(solution)/shard_map/all_to_all | solution.py:150
  72.1 1.9 reshape.341
  73.9 2.2 copy.46
  76.1 2.3 reshape.342
  79.8 2.7 reshape.340
  82.5 2.4 copy.44
  84.9 2.2 dot_general.41
  93.9 1.9 collective-permute-start
  95.9 9.3 %collective-permute-done = bf16[128,768]{1,0:T(8,128)(2,1)S(1)} collective-permute-done((bf16[128,768]{1,0:T(8,128)(2,1)S(1)}, bf16[128,768]{1,0:T(8,128)(2,1)S(1)}, u32[]{:S(2)}, u32[]{:S(2)}) %collective-permute-start) | collective-permute-done | bytes 196640 | tf_op jit(solution)/shard_map/ppermute | solution.py:30
  105.1 1.9 collective-permute-start.1
  108.1 8.3 %collective-permute-done.1 = bf16[128,768]{1,0:T(8,128)(2,1)} collective-permute-done((bf16[128,768]{1,0:T(8,128)(2,1)S(1)}, bf16[128,768]{1,0:T(8,128)(2,1)}, u32[]{:S(2)}, u32[]{:S(2)}) %collective-permute-start.1) | collective-permute-done | bytes 196640 | tf_op jit(solution)/shard_map/ppermute | solution.py:30
  116.4 2.1 collective-permute-start.2
  118.5 2.0 fusion.43
  124.9 2.0 reshape_reshape.9
  126.9 1.7 copy.55
  130.8 2.0 dot_general.51
  138.1 1.9 collective-permute-start.3
  141.0 8.5 %collective-permute-done.3 = bf16[128,768]{1,0:T(8,128)(2,1)S(1)} collective-permute-done((bf16[128,768]{1,0:T(8,128)(2,1)}, bf16[128,768]{1,0:T(8,128)(2,1)S(1)}, u32[]{:S(2)}, u32[]{:S(2)}) %collective-permute-start.3) | collective-permute-done | bytes 196640 | tf_op jit(solution)/shard_map/ppermute | solution.py:30
  149.5 1.9 collective-permute-start.4
  151.4 2.2 convolution_add_fusion.1
  153.6 2.1 copy.53
  156.0 4.8 %collective-permute-done.4 = bf16[128,768]{1,0:T(8,128)(2,1)} collective-permute-done((bf16[128,768]{1,0:T(8,128)(2,1)S(1)}, bf16[128,768]{1,0:T(8,128)(2,1)}, u32[]{:S(2)}, u32[]{:S(2)}) %collective-permute-start.4) | collective-permute-done | bytes 196640 | tf_op jit(solution)/shard_map/ppermute | solution.py:30
  160.8 1.9 collective-permute-start.5
  162.9 9.4 %collective-permute-done.5 = bf16[128,768]{1,0:T(8,128)(2,1)S(1)} collective-permute-done((bf16[128,768]{1,0:T(8,128)(2,1)}, bf16[128,768]{1,0:T(8,128)(2,1)S(1)}, u32[]{:S(2)}, u32[]{:S(2)}) %collective-permute-start.5) | collective-permute-done | bytes 196640 | tf_op jit(solution)/shard_map/ppermute | solution.py:30
  172.2 1.9 collective-permute-start.6
  174.2 9.2 %collective-permute-done.6 = bf16[128,768]{1,0:T(8,128)(2,1)S(1)} collective-permute-done((bf16[128,768]{1,0:T(8,128)(2,1)S(1)}, bf16[128,768]{1,0:T(8,128)(2,1)S(1)}, u32[]{:S(2)}, u32[]{:S(2)}) %collective-permute-start.6) | collective-permute-done | bytes 196640 | tf_op jit(solution)/shard_map/ppermute | solution.py:30
  183.4 1.9 collective-permute-start.7
  187.2 7.4 %collective-permute-done.7 = bf16[128,768]{1,0:T(8,128)(2,1)S(1)} collective-permute-done((bf16[128,768]{1,0:T(8,128)(2,1)S(1)}, bf16[128,768]{1,0:T(8,128)(2,1)S(1)}, u32[]{:S(2)}, u32[]{:S(2)}) %collective-permute-start.7) | collective-permute-done | bytes 196640 | tf_op jit(solution)/shard_map/ppermute | solution.py:30
  194.6 1.9 collective-permute-start.8
  197.5 8.3 %collective-permute-done.8 = bf16[128,768]{1,0:T(8,128)(2,1)S(1)} collective-permute-done((bf16[128,768]{1,0:T(8,128)(2,1)S(1)}, bf16[128,768]{1,0:T(8,128)(2,1)S(1)}, u32[]{:S(2)}, u32[]{:S(2)}) %collective-permute-start.8) | collective-permute-done | bytes 196640 | tf_op jit(solution)/shard_map/ppermute | solution.py:30
  205.8 1.9 collective-permute-start.9
  207.8 9.2 %collective-permute-done.9 = bf16[128,768]{1,0:T(8,128)(2,1)S(1)} collective-permute-done((bf16[128,768]{1,0:T(8,128)(2,1)S(1)}, bf16[128,768]{1,0:T(8,128)(2,1)S(1)}, u32[]{:S(2)}, u32[]{:S(2)}) %collective-permute-start.9) | collective-permute-done | bytes 196640 | tf_op jit(solution)/shard_map/ppermute | solution.py:30
  217.0 1.9 collective-permute-start.10
  219.0 9.2 %collective-permute-done.10 = bf16[128,768]{1,0:T(8,128)(2,1)S(1)} collective-permute-done((bf16[128,768]{1,0:T(8,128)(2,1)S(1)}, bf16[128,768]{1,0:T(8,128)(2,1)S(1)}, u32[]{:S(2)}, u32[]{:S(2)}) %collective-permute-start.10) | collective-permute-done | bytes 196640 | tf_op jit(solution)/shard_map/ppermute | solution.py:30
  228.2 1.9 collective-permute-start.11
  230.2 9.2 %collective-permute-done.11 = bf16[128,768]{1,0:T(8,128)(2,1)S(1)} collective-permute-done((bf16[128,768]{1,0:T(8,128)(2,1)S(1)}, bf16[128,768]{1,0:T(8,128)(2,1)S(1)}, u32[]{:S(2)}, u32[]{:S(2)}) %collective-permute-start.11) | collective-permute-done | bytes 196640 | tf_op jit(solution)/shard_map/ppermute | solution.py:30
  239.4 1.8 fusion.42
  241.2 2.5 copy.50
  243.7 2.5 copy.49
  246.2 9.0 %fusion.2 = (f32[6,3,128]{2,1,0:T(4,128)S(1)}, f32[6,1664,128,3]{2,1,3,0:T(8,128)}) fusion(pred[128,1664]{0,1:T(8,128)(4,1)S(1)} %compare_and_fusion, bf16[1664,6,64,1]{0,2,3,1:T(8,128)(2,1)} %bitcast.102, bf16[128,6,3,64]{0,3,2,1:T(8,128)(2,1)S(1)} %bitcast.106), kind=kOutput, calls=%fused_computation.7 | convolution fusion | flops 502232832 | bytes 17130496 | tf_op jit(solution)/shard_map/qkzr,ckr->kzqc/dot_general | solution.py:203
  255.2 8.6 %fusion = f32[6,3,128]{2,1,0:T(4,128)S(1)} fusion(f32[6,1664,128,3]{2,1,3,0:T(8,128)} %get-tuple-element.17, f32[6,3,128]{2,1,0:T(4,128)S(1)} %get-tuple-element.16, pred[128,1664]{0,1:T(8,128)(4,1)S(1)} %compare_and_fusion), kind=kLoop, calls=%fused_computation.5 | loop fusion | flops 15333120 | bytes 15566848 | tf_op jit(solution)/shard_map/reduce_sum | solution.py:209
  263.9 9.2 %fusion.23 = bf16[128,6,3,64]{0,3,2,1:T(8,128)(2,1)S(1)} fusion(bf16[1664,6,64,1]{0,2,3,1:T(8,128)(2,1)S(1)} %bitcast.110, f32[6,1664,128,3]{2,1,3,0:T(8,128)} %get-tuple-element.17, f32[6,3,128]{2,1,0:T(4,128)S(1)} %get-tuple-element.16, pred[128,1664]{0,1:T(8,128)(4,1)S(1)} %compare_and_fusion, f32[128,6,3]{0,2,1:T(4,128)S(1)} %bitcast.117), kind=kOutput, calls=%fused_computation.34 | convolution fusion | flops 506363904 | bytes 17139712 | tf_op jit(solution)/shard_map/iyxv,vip->xiyp/dot_general | solution.py:211
  (157 shorter events, 39.8 us)
Async XLA Ops:
  0.6 150.8 %copy-start = (bf16[1152,1152]{1,0:T(8,128)(2,1)S(1)}, bf16[1152,1152]{1,0:T(8,128)(2,1)}, u32[]{:S(2)}) copy-start(bf16[1152,1152]{1,0:T(8,128)(2,1)} %param.18) | copy-start | bytes 7962628
  0.6 10.3 %copy-start.27 = (s32[64]{0:T(128)S(1)}, s32[64]{0:T(128)}, u32[]{:S(2)}) copy-start(s32[64]{0:T(128)} %param.27) | copy-start | bytes 772
  0.7 11.0 %copy-start.1 = (s32[64]{0:T(128)S(1)}, s32[64]{0:T(128)}, u32[]{:S(2)}) copy-start(s32[64]{0:T(128)} %param.28) | copy-start | bytes 772
  6.6 19.6 %all-to-all-start = ((bf16[8,8,7680]{2,1,0:T(8,128)(2,1)}), bf16[8,8,7680]{2,1,0:T(8,128)(2,1)}, u32[]{:S(2)}, u32[]{:S(2)}) async-start(bf16[8,8,7680]{2,1,0:T(8,128)(2,1)} %tile.2), calls=%async_computation | async-start | bytes 1966080 | tf_op jit(solution)/shard_map/all_to_all | solution.py:22
  11.6 1.5 copy-start.2
  13.2 2.9 %copy-start.3 = (bf16[128,1152]{1,0:T(8,128)(2,1)S(1)}, bf16[128,1152]{1,0:T(8,128)(2,1)}, u32[]{:S(2)}) copy-start(bf16[128,1152]{1,0:T(8,128)(2,1)} %param.16) | copy-start | bytes 884740
  14.7 16.3 %copy-start.28 = (s32[128]{0:T(128)}, s32[128]{0:T(128)S(1)}, u32[]{:S(2)}) copy-start(s32[128]{0:T(128)S(1)} %iota_add_fusion.1) | copy-start | bytes 1540
  14.7 0.6 copy-start.19
  14.9 30.3 %copy-start.30 = (s32[128]{0:T(128)}, s32[128]{0:T(128)S(1)}, u32[]{:S(2)}) copy-start(s32[128]{0:T(128)S(1)} %broadcast_add_fusion.1) | copy-start | bytes 1540
  36.8 8.3 %copy-start.24 = (bf16[1152]{0:T(1024)(128)(2,1)S(1)}, bf16[1152]{0:T(1024)(128)(2,1)}, u32[]{:S(2)}) copy-start(bf16[1152]{0:T(1024)(128)(2,1)} %param.17) | copy-start | bytes 6916
  36.8 34.3 %all-to-all-start.1 = ((bf16[16,5,7680]{2,1,0:T(8,128)(2,1)}), bf16[16,5,7680]{2,1,0:T(8,128)(2,1)}, u32[]{:S(2)}, u32[]{:S(2)}) async-start(bf16[16,5,7680]{2,1,0:T(8,128)(2,1)} %broadcast_select_fusion), calls=%async_computation.1 | async-start | bytes 3932160 | tf_op jit(solution)/shard_map/all_to_all | solution.py:150
  45.2 41.9 %copy-start.18 = (f32[1152]{0:T(1024)}, f32[1152]{0:T(1024)S(1)}, u32[]{:S(2)}) copy-start(f32[1152]{0:T(1024)S(1)} %convert_element_type.91) | copy-start | bytes 13828
  45.2 41.9 %copy-start.23 = (f32[128]{0:T(128)}, f32[128]{0:T(128)S(1)}, u32[]{:S(2)}) copy-start(f32[128]{0:T(128)S(1)} %add_rsqrt_fusion) | copy-start | bytes 1540
  45.3 41.8 %copy-start.25 = (f32[128,5]{0,1:T(8,128)}, f32[128,5]{0,1:T(8,128)S(1)}, u32[]{:S(2)}) copy-start(f32[128,5]{0,1:T(8,128)S(1)} %fusion.34) | copy-start | bytes 7684
  46.0 45.4 %copy-start.15 = (f32[128,32]{0,1:T(8,128)}, f32[128,32]{0,1:T(8,128)S(1)}, u32[]{:S(2)}) copy-start(f32[128,32]{0,1:T(8,128)S(1)} %get-tuple-element.14) | copy-start | bytes 49156
  87.5 2.1 copy-start.21
  91.4 4.5 %copy-start.22 = (s32[1664]{0:T(1024)S(1)}, s32[1664]{0:T(1024)}, u32[]{:S(2)}) copy-start(s32[1664]{0:T(1024)} %convert_reduce_fusion) | copy-start | bytes 19972
  91.4 15.7 %copy-start.20 = (s32[1664]{0:T(1024)S(1)}, s32[1664]{0:T(1024)}, u32[]{:S(2)}) copy-start(s32[1664]{0:T(1024)} %copy-done.19) | copy-start | bytes 19972
  91.4 15.7 %copy-start.29 = (s32[128]{0:T(128)S(1)}, s32[128]{0:T(128)}, u32[]{:S(2)}) copy-start(s32[128]{0:T(128)} %copy-done.28) | copy-start | bytes 1540
  91.4 15.7 %copy-start.31 = (s32[128]{0:T(128)S(1)}, s32[128]{0:T(128)}, u32[]{:S(2)}) copy-start(s32[128]{0:T(128)} %copy-done.30) | copy-start | bytes 1540
  93.9 22.5 %copy-start.7 = (bf16[128,768]{1,0:T(8,128)(2,1)}, bf16[128,768]{1,0:T(8,128)(2,1)S(1)}, u32[]{:S(2)}) copy-start(bf16[128,768]{1,0:T(8,128)(2,1)S(1)} %pad_maximum_fusion.1) | copy-start | bytes 589828
  93.9 11.2 %collective-permute-start = (bf16[128,768]{1,0:T(8,128)(2,1)S(1)}, bf16[128,768]{1,0:T(8,128)(2,1)S(1)}, u32[]{:S(2)}, u32[]{:S(2)}) collective-permute-start(bf16[128,768]{1,0:T(8,128)(2,1)S(1)} %pad_maximum_fusion.1), channel_id=1, source_target_pairs={{0,1},{1,2},{2,3},{3,4},{4,5},{5,6},{6,7},{7,8},{8,9},{9,10},{10,1... | collective-permute-start | bytes 589832 | tf_op jit(solution)/shard_map/ppermute | solution.py:30
  105.1 11.3 %copy-start.10 = (bf16[128,768]{1,0:T(8,128)(2,1)}, bf16[128,768]{1,0:T(8,128)(2,1)S(1)}, u32[]{:S(2)}) copy-start(bf16[128,768]{1,0:T(8,128)(2,1)S(1)} %collective-permute-done) | copy-start | bytes 589828
  105.1 11.3 %collective-permute-start.1 = (bf16[128,768]{1,0:T(8,128)(2,1)S(1)}, bf16[128,768]{1,0:T(8,128)(2,1)}, u32[]{:S(2)}, u32[]{:S(2)}) collective-permute-start(bf16[128,768]{1,0:T(8,128)(2,1)S(1)} %collective-permute-done), channel_id=1, source_target_pairs={{0,1},{1,2},{2,3},{3,4},{4,5},{5,6},{6,7},{7,8},{8,9},{9,10},{10,1... | collective-permute-start | bytes 589832 | tf_op jit(solution)/shard_map/ppermute | solution.py:30
  116.4 21.6 %collective-permute-start.2 = (bf16[128,768]{1,0:T(8,128)(2,1)}, bf16[128,768]{1,0:T(8,128)(2,1)}, u32[]{:S(2)}, u32[]{:S(2)}) collective-permute-start(bf16[128,768]{1,0:T(8,128)(2,1)} %collective-permute-done.1), channel_id=1, source_target_pairs={{0,1},{1,2},{2,3},{3,4},{4,5},{5,6},{6,7},{7,8},{8,9},{9,10},{10,1... | collective-permute-start | bytes 589832 | tf_op jit(solution)/shard_map/ppermute | solution.py:30
  138.1 11.4 %collective-permute-start.3 = (bf16[128,768]{1,0:T(8,128)(2,1)}, bf16[128,768]{1,0:T(8,128)(2,1)S(1)}, u32[]{:S(2)}, u32[]{:S(2)}) collective-permute-start(bf16[128,768]{1,0:T(8,128)(2,1)} %collective-permute-done.2), channel_id=1, source_target_pairs={{0,1},{1,2},{2,3},{3,4},{4,5},{5,6},{6,7},{7,8},{8,9},{9,10},{10,1... | collective-permute-start | bytes 589832 | tf_op jit(solution)/shard_map/ppermute | solution.py:30
  141.0 14.8 %copy-start.8 = (bf16[128,768]{1,0:T(8,128)(2,1)S(1)}, bf16[128,768]{1,0:T(8,128)(2,1)}, u32[]{:S(2)}) copy-start(bf16[128,768]{1,0:T(8,128)(2,1)} %copy-done.7) | copy-start | bytes 589828
  149.5 6.2 %copy-start.12 = (bf16[128,768]{1,0:T(8,128)(2,1)}, bf16[128,768]{1,0:T(8,128)(2,1)S(1)}, u32[]{:S(2)}) copy-start(bf16[128,768]{1,0:T(8,128)(2,1)S(1)} %collective-permute-done.3) | copy-start | bytes 589828
  149.5 11.3 %collective-permute-start.4 = (bf16[128,768]{1,0:T(8,128)(2,1)S(1)}, bf16[128,768]{1,0:T(8,128)(2,1)}, u32[]{:S(2)}, u32[]{:S(2)}) collective-permute-start(bf16[128,768]{1,0:T(8,128)(2,1)S(1)} %collective-permute-done.3), channel_id=1, source_target_pairs={{0,1},{1,2},{2,3},{3,4},{4,5},{5,6},{6,7},{7,8},{8,9},{9,10},{10,1... | collective-permute-start | bytes 589832 | tf_op jit(solution)/shard_map/ppermute | solution.py:30
  155.8 7.0 %copy-start.5 = (f32[128,1152]{0,1:T(8,128)S(1)}, f32[128,1152]{0,1:T(8,128)}, u32[]{:S(2)}) copy-start(f32[128,1152]{0,1:T(8,128)} %copy.53) | copy-start | bytes 1769476
  155.8 7.0 %copy-start.16 = (f32[128,32]{0,1:T(8,128)S(1)}, f32[128,32]{0,1:T(8,128)}, u32[]{:S(2)}) copy-start(f32[128,32]{0,1:T(8,128)} %copy-done.15) | copy-start | bytes 49156
  155.8 7.0 %copy-start.17 = (f32[128,32]{0,1:T(8,128)S(1)}, f32[128,32]{0,1:T(8,128)}, u32[]{:S(2)}) copy-start(f32[128,32]{0,1:T(8,128)} %get-tuple-element.15) | copy-start | bytes 49156
  155.8 18.4 %copy-start.11 = (bf16[128,768]{1,0:T(8,128)(2,1)S(1)}, bf16[128,768]{1,0:T(8,128)(2,1)}, u32[]{:S(2)}) copy-start(bf16[128,768]{1,0:T(8,128)(2,1)} %copy-done.10) | copy-start | bytes 589828
  156.0 40.6 %copy-start.13 = (bf16[128,768]{1,0:T(8,128)(2,1)S(1)}, bf16[128,768]{1,0:T(8,128)(2,1)}, u32[]{:S(2)}) copy-start(bf16[128,768]{1,0:T(8,128)(2,1)} %copy-done.12) | copy-start | bytes 589828
  160.8 11.4 %collective-permute-start.5 = (bf16[128,768]{1,0:T(8,128)(2,1)}, bf16[128,768]{1,0:T(8,128)(2,1)S(1)}, u32[]{:S(2)}, u32[]{:S(2)}) collective-permute-start(bf16[128,768]{1,0:T(8,128)(2,1)} %collective-permute-done.4), channel_id=1, source_target_pairs={{0,1},{1,2},{2,3},{3,4},{4,5},{5,6},{6,7},{7,8},{8,9},{9,10},{10,1... | collective-permute-start | bytes 589832 | tf_op jit(solution)/shard_map/ppermute | solution.py:30
  172.2 11.2 %collective-permute-start.6 = (bf16[128,768]{1,0:T(8,128)(2,1)S(1)}, bf16[128,768]{1,0:T(8,128)(2,1)S(1)}, u32[]{:S(2)}, u32[]{:S(2)}) collective-permute-start(bf16[128,768]{1,0:T(8,128)(2,1)S(1)} %collective-permute-done.5), channel_id=1, source_target_pairs={{0,1},{1,2},{2,3},{3,4},{4,5},{5,6},{6,7},{7,8},{8,9},{9,10},{10,1... | collective-permute-start | bytes 589832 | tf_op jit(solution)/shard_map/ppermute | solution.py:30
  183.4 11.2 %collective-permute-start.7 = (bf16[128,768]{1,0:T(8,128)(2,1)S(1)}, bf16[128,768]{1,0:T(8,128)(2,1)S(1)}, u32[]{:S(2)}, u32[]{:S(2)}) collective-permute-start(bf16[128,768]{1,0:T(8,128)(2,1)S(1)} %collective-permute-done.6), channel_id=1, source_target_pairs={{0,1},{1,2},{2,3},{3,4},{4,5},{5,6},{6,7},{7,8},{8,9},{9,10},{10,1... | collective-permute-start | bytes 589832 | tf_op jit(solution)/shard_map/ppermute | solution.py:30
  194.6 11.2 %collective-permute-start.8 = (bf16[128,768]{1,0:T(8,128)(2,1)S(1)}, bf16[128,768]{1,0:T(8,128)(2,1)S(1)}, u32[]{:S(2)}, u32[]{:S(2)}) collective-permute-start(bf16[128,768]{1,0:T(8,128)(2,1)S(1)} %collective-permute-done.7), channel_id=1, source_target_pairs={{0,1},{1,2},{2,3},{3,4},{4,5},{5,6},{6,7},{7,8},{8,9},{9,10},{10,1... | collective-permute-start | bytes 589832 | tf_op jit(solution)/shard_map/ppermute | solution.py:30
  205.8 11.2 %collective-permute-start.9 = (bf16[128,768]{1,0:T(8,128)(2,1)S(1)}, bf16[128,768]{1,0:T(8,128)(2,1)S(1)}, u32[]{:S(2)}, u32[]{:S(2)}) collective-permute-start(bf16[128,768]{1,0:T(8,128)(2,1)S(1)} %collective-permute-done.8), channel_id=1, source_target_pairs={{0,1},{1,2},{2,3},{3,4},{4,5},{5,6},{6,7},{7,8},{8,9},{9,10},{10,1... | collective-permute-start | bytes 589832 | tf_op jit(solution)/shard_map/ppermute | solution.py:30
  217.0 11.2 %collective-permute-start.10 = (bf16[128,768]{1,0:T(8,128)(2,1)S(1)}, bf16[128,768]{1,0:T(8,128)(2,1)S(1)}, u32[]{:S(2)}, u32[]{:S(2)}) collective-permute-start(bf16[128,768]{1,0:T(8,128)(2,1)S(1)} %collective-permute-done.9), channel_id=1, source_target_pairs={{0,1},{1,2},{2,3},{3,4},{4,5},{5,6},{6,7},{7,8},{8,9},{9,10},{10,1... | collective-permute-start | bytes 589832 | tf_op jit(solution)/shard_map/ppermute | solution.py:30
  228.2 11.2 %collective-permute-start.11 = (bf16[128,768]{1,0:T(8,128)(2,1)S(1)}, bf16[128,768]{1,0:T(8,128)(2,1)S(1)}, u32[]{:S(2)}, u32[]{:S(2)}) collective-permute-start(bf16[128,768]{1,0:T(8,128)(2,1)S(1)} %collective-permute-done.10), channel_id=1, source_target_pairs={{0,1},{1,2},{2,3},{3,4},{4,5},{5,6},{6,7},{7,8},{8,9},{9,10},{10,1... | collective-permute-start | bytes 589832 | tf_op jit(solution)/shard_map/ppermute | solution.py:30
  255.2 8.6 %copy-start.6 = (bf16[1664,384]{0,1:T(8,128)(2,1)S(1)}, bf16[1664,384]{0,1:T(8,128)(2,1)}, u32[]{:S(2)}) copy-start(bf16[1664,384]{0,1:T(8,128)(2,1)} %copy.49) | copy-start | bytes 3833860
  263.8 9.3 %copy-start.14 = (bf16[5,16,1152]{2,1,0:T(8,128)(2,1)S(1)}, bf16[5,16,1152]{2,1,0:T(8,128)(2,1)}, u32[]{:S(2)}) copy-start(bf16[5,16,1152]{2,1,0:T(8,128)(2,1)} %dot_general.51) | copy-start | bytes 552964
  263.8 9.3 %copy-start.26 = (f32[128,5]{0,1:T(8,128)S(1)}, f32[128,5]{0,1:T(8,128)}, u32[]{:S(2)}) copy-start(f32[128,5]{0,1:T(8,128)} %copy-done.25) | copy-start | bytes 7684
  263.9 9.5 %copy-start.9 = (bf16[80,1152]{1,0:T(8,128)(2,1)S(1)}, bf16[80,1152]{1,0:T(8,128)(2,1)}, u32[]{:S(2)}) copy-start(bf16[80,1152]{1,0:T(8,128)(2,1)} %reshape_reshape.9) | copy-start | bytes 552964
  263.9 9.7 %copy-start.4 = (bf16[1152,1152]{1,0:T(8,128)(2,1)S(1)}, bf16[1152,1152]{1,0:T(8,128)(2,1)}, u32[]{:S(2)}) copy-start(bf16[1152,1152]{1,0:T(8,128)(2,1)} %param.21) | copy-start | bytes 7962628
